TPU v7x, 256 devices: a whole 4x4x8 slice. The times are simulated.
256 devices in a mesh: dp: 32 (over z_lo, y, core), graph: 8 (over z_hi, x).
Axes of the slice: x: 4, y: 4, z: 8 (z_hi: 2, z_lo: 4; z = z_hi * 4 + z_lo), core: 2. Of those that a mesh axis runs over, the one named last changes fastest.
Arguments:
- embedding: bfloat16 [32, 12288, 512], P('dp', 'graph'), may hold values from -6 to 6
- triplet_basis: bfloat16 [32, 49152, 64], P('dp', 'graph'), may hold values from -6 to 6
- atom_cotangent: bfloat16 [32, 768, 1024], P('dp', 'graph'), may hold values from -6 to 6
- fidelity: int32 [32, 768], P('dp', 'graph'), may hold values 0 or 1
- edge_target: int32 [32, 12288], P('dp', 'graph'), may hold values from 0 to 767, as said below
- triplet_source: int32 [32, 49152], P('dp', 'graph'), may hold values from 0 to 12287, as said below
- triplet_target: int32 [32, 49152], P('dp', 'graph'), may hold values from 0 to 12287, as said below
- edge_count: int32 [32, 8], P('dp', 'graph'), may hold values from 768 to 1536, as said below
- triplet_count: int32 [32, 8], P('dp', 'graph'), may hold values from 1536 to 6144, as said below
- w_down: bfloat16 [512, 64], replicated, may hold values from -0.25 to 0.25
- w_up: bfloat16 [64, 512], replicated, may hold values from -0.75 to 0.75
- w_atom: bfloat16 [512, 1024], replicated, may hold values from -0.25 to 0.25
Outputs:
- embedding_grad: bfloat16 [32, 12288, 512], P('dp', 'graph')
- w_atom_grad: float32 [512, 1024], P(None, 'graph')
- w_up_grad: float32 [64, 512], replicated
- w_down_grad: float32 [512, 64], replicated
Inputs may be any that keep to these rules, and one draw needn't show every extreme that they name: `edge_target`: edges of index g of graph, slots g * 1536 to (g + 1) * 1536 - 1, have target atoms anywhere in their batch. `triplet_source`: A live edge slot of any index of graph in the same batch. `triplet_target`: A live edge slot of the same index of graph as the triplet slot. `edge_count`: some index of graph of every batch has all 1536 edge slots live. `triplet_count`: some index of graph of every batch has all 6144 triplet slots live.
All inputs are finite; a program needn't handle non-finite values. No bound on the sum of `fidelity` on one device may be relied on, other than what follows from the above.
Results may differ from a plain program's by a relative error of at most 0.0077.
Values may be sent and summed in bfloat16 or wider, within the bound.
No kernel may reach another device: no remote copies, remote signals or barrier semaphores. Data moves between devices by JAX's collectives and lax.ppermute only.
A program may use at most 128 MiB of HBM per device.

v0:
```python
import jax
import jax.numpy as jnp
from jax import lax
from jax.sharding import PartitionSpec as P


def local(
    embedding,
    triplet_basis,
    atom_cotangent,
    fidelity,
    edge_target,
    triplet_source,
    triplet_target,
    edge_count,
    triplet_count,
    w_down,
    w_up,
    w_atom,
):
    rows = embedding[0]
    basis = triplet_basis[0]
    edge_slots = rows.shape[0]
    trip_slots = basis.shape[0]
    groups = lax.axis_size("graph")
    here = lax.axis_index("graph")
    edge_live = jnp.arange(edge_slots, dtype=jnp.int32) < edge_count[0, 0]
    trip_live = jnp.arange(trip_slots, dtype=jnp.int32) < triplet_count[0, 0]
    weight = 1.0 + 3.0 * fidelity[0].astype(jnp.float32)
    scaled = (weight[:, None] * atom_cotangent[0].astype(jnp.float32)).astype(jnp.bfloat16)
    atoms_all = lax.all_gather(scaled, "graph", axis=0, tiled=True)
    projected = jnp.dot(rows, w_down, preferred_element_type=jnp.float32).astype(jnp.bfloat16)
    table = lax.all_gather(projected, "graph", axis=0, tiled=True)
    feats = jnp.take(table, triplet_source[0], axis=0)
    local_dest = triplet_target[0] - here * edge_slots
    product = jnp.where(
        trip_live[:, None], feats.astype(jnp.float32) * basis.astype(jnp.float32), jnp.float32(0.0)
    )
    aggregate = jax.ops.segment_sum(product, local_dest, num_segments=edge_slots).astype(
        jnp.bfloat16
    )
    pre = jnp.dot(aggregate, w_up, preferred_element_type=jnp.float32)
    sig = jax.nn.sigmoid(pre)
    updated = (rows.astype(jnp.float32) + pre * sig).astype(jnp.bfloat16)
    edge_in = jnp.where(
        edge_live[:, None], jnp.take(atoms_all, edge_target[0], axis=0), jnp.zeros((), jnp.bfloat16)
    )
    edge_out = jnp.dot(edge_in, w_atom.T, preferred_element_type=jnp.float32)
    part_atom = jnp.dot(updated.T, edge_in, preferred_element_type=jnp.float32)
    pre_grad = (edge_out * sig * (1.0 + pre * (1.0 - sig))).astype(jnp.bfloat16)
    part_up = jnp.dot(aggregate.T, pre_grad, preferred_element_type=jnp.float32)
    aggregate_grad = jnp.dot(pre_grad, w_up.T, preferred_element_type=jnp.float32).astype(
        jnp.bfloat16
    )
    contrib = jnp.where(
        trip_live[:, None],
        jnp.take(aggregate_grad, local_dest, axis=0).astype(jnp.float32)
        * basis.astype(jnp.float32),
        jnp.float32(0.0),
    )
    partial_grad = jax.ops.segment_sum(
        contrib, triplet_source[0], num_segments=edge_slots * groups
    ).astype(jnp.bfloat16)
    source_grad = (
        lax.psum_scatter(partial_grad, "graph", scatter_dimension=0, tiled=True)
        .astype(jnp.float32)
        .astype(jnp.bfloat16)
    )
    part_down = jnp.dot(rows.T, source_grad, preferred_element_type=jnp.float32)
    result = (edge_out + jnp.dot(source_grad, w_down.T, preferred_element_type=jnp.float32)).astype(
        jnp.bfloat16
    )
    total_atom, up_grad, down_grad = lax.psum((part_atom, part_up, part_down), ("dp", "graph"))
    width = total_atom.shape[1] // groups
    atom_grad = lax.dynamic_slice_in_dim(total_atom, here * width, width, 1)
    return (result[None], atom_grad, up_grad, down_grad)


def solution(mesh):
    return jax.shard_map(
        local,
        mesh=mesh,
        in_specs=(
            P("dp", "graph", None),
            P("dp", "graph", None),
            P("dp", "graph", None),
            P("dp", "graph"),
            P("dp", "graph"),
            P("dp", "graph"),
            P("dp", "graph"),
            P("dp", "graph"),
            P("dp", "graph"),
            P(),
            P(),
            P(),
        ),
        out_specs=(P("dp", "graph", None), P(None, "graph"), P(), P()),
        check_vma=False,
    )
```

profile of v0, /device:TPU:8, one launch (start us, length us, event | category | flops | bytes accessed | tf_op | source)
XLA Modules:
  0.0 701.8 jit_solution(8970966009916328786)
XLA Ops:
  8.0 1.7 fusion.30
  9.8 2.7 convolution_convert_fusion.1
  16.7 0.9 copy.30
  17.7 65.4 %all-gather.3.cloned.1.call-done = bf16[768,1024]{1,0:T(8,128)(2,1)} async-done(((bf16[96,1024]{1,0:T(8,128)(2,1)}), bf16[768,1024]{1,0:T(8,128)(2,1)}) %all-gather.3.cloned.1.call-update) | async-done | bytes 1572880 | tf_op jit(solution)/shard_map/all_gather | solution.py:31
  83.1 9.4 %gather_fusion = bf16[1536,1024]{1,0:T(8,128)(2,1)} fusion(bf16[768,1024]{1,0:T(8,128)(2,1)} %all-gather.3.cloned.1.call-done, s32[2048]{0:T(1024)S(1)} %pad_clamp_fusion), kind=kCustom, calls=%fused_computation | custom fusion | bytes 6297600 | tf_op jit(solution)/shard_map/jit(_take)/gather | solution.py:46
  92.5 5.5 fusion.40
  98.0 52.9 %all-gather.5.cloned.1.call-done = bf16[12288,64]{0,1:T(8,128)(2,1)} async-done(((bf16[1536,64]{0,1:T(8,128)(2,1)}), bf16[12288,64]{0,1:T(8,128)(2,1)}) %all-gather.5.cloned.1.call-update) | async-done | bytes 1572880 | tf_op jit(solution)/shard_map/all_gather | solution.py:33
  150.9 4.1 copy.29
  155.0 74.9 %scatter_custom_fusion = f32[1536,64]{1,0:T(8,128)S(1)} fusion(s32[6144]{0:T(1024)S(1)} %bitcast.56, bf16[1,6144,64]{2,1,0:T(8,128)(2,1)S(1)} %copy.30, f32[]{:T(128)} %constant.38.clone.1, pred[6144]{0:T(1024)(128)(4,1)S(1)} %get-tuple-element.14, pred[6144]{0:T(1024)(128)(4,1)S(1)} %get-tuple-element.13, bf16[]{:T(256)} %constant.30.clone.1, ...), kind=kCustom, calls=%fused_computation.9 | custom fusion | flops 2359296 | bytes 5150208 | tf_op jit(solution)/shard_map/scatter-add | solution.py:39
  230.0 5.0 multiply_convert_fusion
  235.0 1.1 copy-done.2
  236.2 1.3 convolution_convert_fusion
  237.4 1.8 copy.31
  239.3 77.7 %scatter_custom_fusion.1 = f32[12288,64]{1,0:T(8,128)} fusion(s32[6144]{0:T(1024)S(1)} %bitcast.52, f32[]{:T(128)} %constant.38.clone.1, bf16[1,6144,64]{2,1,0:T(8,128)(2,1)S(1)} %copy.30, pred[6144]{0:T(1024)(128)(4,1)S(1)} %compare_and_fusion.1, pred[6144]{0:T(1024)(128)(4,1)S(1)} %get-tuple-element.13, bf16[]{:T(256)} %constant.30.clone.1, ...), kind=kCustom, calls=%fused_computation.11 | custom fusion | flops 2359296 | bytes 5150208 | tf_op jit(solution)/shard_map/scatter-add | solution.py:61
  317.0 4.2 convert_element_type.68
  321.2 2.6 fusion.32
  323.8 6.4 fusion.20
  330.2 94.1 %reduce-scatter.2.cloned.1.call-done = bf16[1536,64]{1,0:T(8,128)(2,1)} async-done(((bf16[12288,64]{1,0:T(8,128)(2,1)}), bf16[1536,64]{1,0:T(8,128)(2,1)}) %reduce-scatter.2.cloned.1.call-update) | async-done | bytes 196624 | tf_op jit(solution)/shard_map/reduce_scatter | solution.py:65
  424.3 2.1 fusion.25
  426.5 3.6 fusion.10
  430.1 260.4 %all-reduce.3.cloned.1.call-done = (f32[512,1024]{1,0:T(8,128)}, f32[64,512]{1,0:T(8,128)}, f32[512,64]{0,1:T(8,128)}) async-done(((f32[512,1024]{1,0:T(8,128)}, f32[64,512]{1,0:T(8,128)}, f32[512,64]{0,1:T(8,128)}), (f32[512,1024]{1,0:T(8,128)}, f32[64,512]{1,0:T(8,128)}, f32[512,64]{0,1:T(8,128)})) %all-reduce.3.cloned.1.call-update) | async-done | bytes 2359312 | tf_op jit(solution)/shard_map/psum | solution.py:73
  690.5 1.7 constant_dynamic-slice_fusion
  692.2 1.6 copy.37
  693.7 1.6 copy.38
  (38 shorter events, 3.9 us)
Async XLA Ops:
  7.2 85.3 %copy-start = (bf16[512,1024]{1,0:T(8,128)(2,1)S(1)}, bf16[512,1024]{1,0:T(8,128)(2,1)}, u32[]{:S(2)}) copy-start(bf16[512,1024]{1,0:T(8,128)(2,1)} %param.23) | copy-start | bytes 3145732
  7.2 9.5 %copy-start.4 = (bf16[1,6144,64]{1,2,0:T(8,128)(2,1)S(1)}, bf16[1,6144,64]{1,2,0:T(8,128)(2,1)}, u32[]{:S(2)}) copy-start(bf16[1,6144,64]{1,2,0:T(8,128)(2,1)} %param.13) | copy-start | bytes 2359300
  7.2 10.4 %copy-start.6 = (s32[1,6144]{1,0:T(1,128)S(1)}, s32[1,6144]{1,0:T(1,128)}, u32[]{:S(2)}) copy-start(s32[1,6144]{1,0:T(1,128)} %param.17) | copy-start | bytes 73732
  7.2 75.9 %all-gather.3.cloned.1.call-start = ((), (), s32[]{:S(2)}) async-start(), calls=%async_computation.1 | async-start | bytes 1769472 | tf_op jit(solution)/shard_map/all_gather | solution.py:31
  9.8 141.2 %all-gather.5.cloned.1.call-start = ((), (), s32[]{:S(2)}) async-start(), calls=%async_computation.2 | async-start | bytes 1769472 | tf_op jit(solution)/shard_map/all_gather | solution.py:33
  12.5 411.8 %reduce-scatter.2.cloned.1.call-start = ((), (), s32[]{:S(2)}) async-start(), calls=%async_computation.3 | async-start | bytes 3538944 | tf_op jit(solution)/shard_map/reduce_scatter | solution.py:65
  17.7 74.8 %copy-start.8 = (pred[1536]{0:T(1024)(128)(4,1)S(1)}, pred[1536]{0:T(1024)(128)(4,1)}, u32[]{:S(2)}) copy-start(pred[1536]{0:T(1024)(128)(4,1)} %get-tuple-element.11) | copy-start | bytes 4612
  17.7 74.8 %copy-start.9 = (pred[1536]{0:T(1024)(128)(4,1)S(1)}, pred[1536]{0:T(1024)(128)(4,1)}, u32[]{:S(2)}) copy-start(pred[1536]{0:T(1024)(128)(4,1)} %get-tuple-element.12) | copy-start | bytes 4612
  230.0 6.2 copy-start.7
  235.0 1.1 copy-start.2
  321.1 2.7 copy-start.1
  321.2 369.3 %all-reduce.3.cloned.1.call-start = ((), (), s32[]{:S(2)}) async-start(), calls=%async_computation.4 | async-start | bytes 4718592 | tf_op jit(solution)/shard_map/psum | solution.py:73
  330.2 96.3 %copy-start.5 = (bf16[512,64]{0,1:T(8,128)(2,1)S(1)}, bf16[512,64]{0,1:T(8,128)(2,1)}, u32[]{:S(2)}) copy-start(bf16[512,64]{0,1:T(8,128)(2,1)} %param.21) | copy-start | bytes 196612
  424.3 2.2 copy-start.3
Sparse Core Ops, SparseCore 0:
  11.2 71.8 all-gather.2
  86.2 64.6 all-gather.4
  321.3 102.9 reduce-scatter.1
  430.4 259.9 all-reduce.2
where the time goes:
time: 703 us; the launch traced here: 702 us
  waiting for transfers between devices  473 us (67%)
  other arithmetic  162 us (23%)
  matrix products  29.2 us (4%)
  local copies, waits for them, and re-layouts  22.2 us (3%)
  between operations  15.2 us (2%)
    psum x1, waiting for transfers between devices, local(): lax.psum((part_atom, part_up, part_down), ('dp', 'graph'))  260 us
    reduce_scatter x1, waiting for transfers between devices, local(): lax.psum_scatter(partial_grad, 'graph', scatter_dimension=0, tiled=True)  94.1 us
    scatter-add x1, other arithmetic, local(): jax.ops.segment_sum(contrib, triplet_source[0], num_segments=edge_slots *...  77.7 us
    scatter-add x1, other arithmetic, local(): jax.ops.segment_sum(product, local_dest, num_segments=edge_slots)  74.9 us
    all_gather x1, waiting for transfers between devices, local(): atoms_all = lax.all_gather(scaled, 'graph', axis=0, tiled=True)  65.4 us
    all_gather x1, waiting for transfers between devices, local(): table = lax.all_gather(projected, 'graph', axis=0, tiled=True)  52.9 us
  transfers between devices with their start and end apart: 4, of which 4 were waited for; matrix products, arithmetic and copies ran while one was open for 5% of the time, Pallas kernels for 0%

commit v1 on v0

--- a/solution.py
+++ b/solution.py
@@ -30,7 +30,8 @@
     scaled = (weight[:, None] * atom_cotangent[0].astype(jnp.float32)).astype(jnp.bfloat16)
     atoms_all = lax.all_gather(scaled, "graph", axis=0, tiled=True)
     projected = jnp.dot(rows, w_down, preferred_element_type=jnp.float32).astype(jnp.bfloat16)
-    table = lax.all_gather(projected, "graph", axis=0, tiled=True)
+    z2 = jnp.stack([projected] * jax.lax.axis_size("graph"))
+    table = jnp.concatenate(jax.lax.all_to_all(z2, "graph", 0, 0), axis=0)
     feats = jnp.take(table, triplet_source[0], axis=0)
     local_dest = triplet_target[0] - here * edge_slots
     product = jnp.where(

time: 703 us -> 665 us (0.946)
  waiting for transfers between devices: 473 us -> 425 us
  starting transfers between devices: 0.16 us -> 11.2 us
    all_gather x1 -> x0, waiting for transfers between devices: 52.9 us -> none  [local(): table = lax.all_gather(projected, 'graph', axis=0, tiled=True)]
    all_to_all x0 -> x1, starting transfers between devices: none -> 11.1 us  [local(): table = jnp.concatenate(jax.lax.all_to_all(z2, 'graph', 0, 0), axis=0)]
  transfers between devices with their start and end apart: 4 -> 4, of which waited for: 4 -> 3; matrix products, arithmetic and copies ran while one was open for 5% -> 5% of each run, Pallas kernels for 0% -> 0%
where the time goes in v1:
time: 665 us; the launch traced here: 664 us
  waiting for transfers between devices  425 us (64%)
  other arithmetic  160 us (24%)
  matrix products  28.5 us (4%)
  local copies, waits for them, and re-layouts  23.5 us (4%)
  between operations  15.2 us (2%)
  starting transfers between devices  11.2 us (2%)
    psum x1, waiting for transfers between devices, local(): lax.psum((part_atom, part_up, part_down), ('dp', 'graph'))  261 us
    reduce_scatter x1, waiting for transfers between devices, local(): lax.psum_scatter(partial_grad, 'graph', scatter_dimension=0, tiled=True)  96.8 us
    scatter-add x1, other arithmetic, local(): jax.ops.segment_sum(contrib, triplet_source[0], num_segments=edge_slots *...  77.6 us
    scatter-add x1, other arithmetic, local(): jax.ops.segment_sum(product, local_dest, num_segments=edge_slots)  75 us
    all_gather x1, waiting for transfers between devices, local(): atoms_all = lax.all_gather(scaled, 'graph', axis=0, tiled=True)  67.8 us
  transfers between devices with their start and end apart: 4, of which 3 were waited for; matrix products, arithmetic and copies ran while one was open for 5% of the time, Pallas kernels for 0%

profile of v1, /device:TPU:8, one launch (start us, length us, event | category | flops | bytes accessed | tf_op | source)
XLA Modules:
  0.0 663.7 jit_solution(7014523695578359783)
XLA Ops:
  8.0 1.7 fusion.30
  9.7 2.1 convolution_convert_fusion.1
  11.8 1.3 stack.2
  13.1 11.1 %all-to-all-start = ((bf16[8,1536,64]{1,2,0:T(8,128)(2,1)}), bf16[8,1536,64]{1,2,0:T(8,128)(2,1)}, u32[]{:S(2)}, u32[]{:S(2)}) async-start(bf16[8,1536,64]{1,2,0:T(8,128)(2,1)} %stack.2), calls=%async_computation | async-start | bytes 3145728 | tf_op jit(solution)/shard_map/all_to_all | solution.py:34
  27.2 67.8 %all-gather.2.cloned.1.call-done = bf16[768,1024]{1,0:T(8,128)(2,1)} async-done(((bf16[96,1024]{1,0:T(8,128)(2,1)}), bf16[768,1024]{1,0:T(8,128)(2,1)}) %all-gather.2.cloned.1.call-update) | async-done | bytes 1572880 | tf_op jit(solution)/shard_map/all_gather | solution.py:31
  95.1 9.4 %gather_fusion = bf16[1536,1024]{1,0:T(8,128)(2,1)} fusion(bf16[768,1024]{1,0:T(8,128)(2,1)} %all-gather.2.cloned.1.call-done, s32[2048]{0:T(1024)S(1)} %pad_clamp_fusion), kind=kCustom, calls=%fused_computation | custom fusion | bytes 6297600 | tf_op jit(solution)/shard_map/jit(_take)/gather | solution.py:47
  104.5 5.5 fusion.40
  109.9 4.1 copy.32
  114.1 75.0 %scatter_custom_fusion = f32[1536,64]{1,0:T(8,128)S(1)} fusion(s32[6144]{0:T(1024)S(1)} %bitcast.58, bf16[1,6144,64]{2,1,0:T(8,128)(2,1)S(1)} %copy.33, f32[]{:T(128)} %constant.38.clone.1, pred[6144]{0:T(1024)(128)(4,1)S(1)} %get-tuple-element.14, pred[6144]{0:T(1024)(128)(4,1)S(1)} %get-tuple-element.13, bf16[]{:T(256)} %constant.30.clone.1, ...), kind=kCustom, calls=%fused_computation.9 | custom fusion | flops 2359296 | bytes 5150208 | tf_op jit(solution)/shard_map/scatter-add | solution.py:40
  189.0 5.0 multiply_convert_fusion
  194.1 1.1 copy-done.2
  195.2 1.3 convolution_convert_fusion
  196.5 1.9 copy.34
  198.3 77.6 %scatter_custom_fusion.1 = f32[12288,64]{1,0:T(8,128)} fusion(s32[6144]{0:T(1024)S(1)} %bitcast.54, f32[]{:T(128)} %constant.38.clone.1, bf16[1,6144,64]{2,1,0:T(8,128)(2,1)S(1)} %copy.33, pred[6144]{0:T(1024)(128)(4,1)S(1)} %compare_and_fusion.1, pred[6144]{0:T(1024)(128)(4,1)S(1)} %get-tuple-element.13, bf16[]{:T(256)} %constant.30.clone.1, ...), kind=kCustom, calls=%fused_computation.11 | custom fusion | flops 2359296 | bytes 5150208 | tf_op jit(solution)/shard_map/scatter-add | solution.py:62
  276.0 4.2 convert_element_type.68
  280.2 2.6 fusion.32
  282.8 6.4 fusion.20
  289.2 96.8 %reduce-scatter.2.cloned.1.call-done = bf16[1536,64]{1,0:T(8,128)(2,1)} async-done(((bf16[12288,64]{1,0:T(8,128)(2,1)}), bf16[1536,64]{1,0:T(8,128)(2,1)}) %reduce-scatter.2.cloned.1.call-update) | async-done | bytes 196624 | tf_op jit(solution)/shard_map/reduce_scatter | solution.py:66
  386.0 2.1 fusion.25
  388.2 3.6 fusion.10
  391.8 260.6 %all-reduce.3.cloned.1.call-done = (f32[512,1024]{1,0:T(8,128)}, f32[64,512]{1,0:T(8,128)}, f32[512,64]{0,1:T(8,128)}) async-done(((f32[512,1024]{1,0:T(8,128)}, f32[64,512]{1,0:T(8,128)}, f32[512,64]{0,1:T(8,128)}), (f32[512,1024]{1,0:T(8,128)}, f32[64,512]{1,0:T(8,128)}, f32[512,64]{0,1:T(8,128)})) %all-reduce.3.cloned.1.call-update) | async-done | bytes 2359312 | tf_op jit(solution)/shard_map/psum | solution.py:74
  652.4 1.7 constant_dynamic-slice_fusion
  654.1 1.6 copy.40
  655.6 1.6 copy.41
  (42 shorter events, 2.6 us)
Async XLA Ops:
  7.2 97.3 %copy-start = (bf16[512,1024]{1,0:T(8,128)(2,1)S(1)}, bf16[512,1024]{1,0:T(8,128)(2,1)}, u32[]{:S(2)}) copy-start(bf16[512,1024]{1,0:T(8,128)(2,1)} %param.23) | copy-start | bytes 3145732
  7.2 87.9 %all-gather.2.cloned.1.call-start = ((), (), s32[]{:S(2)}) async-start(), calls=%async_computation.2 | async-start | bytes 1769472 | tf_op jit(solution)/shard_map/all_gather | solution.py:31
  9.7 14.5 %copy-start.9 = (s32[1,6144]{1,0:T(1,128)S(1)}, s32[1,6144]{1,0:T(1,128)}, u32[]{:S(2)}) copy-start(s32[1,6144]{1,0:T(1,128)} %param.18) | copy-start | bytes 73732
  9.7 15.2 %copy-start.8 = (s32[1,1536]{1,0:T(1,128)S(1)}, s32[1,1536]{1,0:T(1,128)}, u32[]{:S(2)}) copy-start(s32[1,1536]{1,0:T(1,128)} %param.16) | copy-start | bytes 18436
  9.7 16.5 %copy-start.4 = (bf16[1,6144,64]{1,2,0:T(8,128)(2,1)S(1)}, bf16[1,6144,64]{1,2,0:T(8,128)(2,1)}, u32[]{:S(2)}) copy-start(bf16[1,6144,64]{1,2,0:T(8,128)(2,1)} %param.13) | copy-start | bytes 2359300
  13.1 14.0 %copy-start.6 = (s32[1,6144]{1,0:T(1,128)S(1)}, s32[1,6144]{1,0:T(1,128)}, u32[]{:S(2)}) copy-start(s32[1,6144]{1,0:T(1,128)} %param.17) | copy-start | bytes 73732
  13.1 96.8 %all-to-all-start = ((bf16[8,1536,64]{1,2,0:T(8,128)(2,1)}), bf16[8,1536,64]{1,2,0:T(8,128)(2,1)}, u32[]{:S(2)}, u32[]{:S(2)}) async-start(bf16[8,1536,64]{1,2,0:T(8,128)(2,1)} %stack.2), calls=%async_computation | async-start | bytes 3145728 | tf_op jit(solution)/shard_map/all_to_all | solution.py:34
  24.1 361.9 %reduce-scatter.2.cloned.1.call-start = ((), (), s32[]{:S(2)}) async-start(), calls=%async_computation.3 | async-start | bytes 3538944 | tf_op jit(solution)/shard_map/reduce_scatter | solution.py:66
  27.2 77.2 %copy-start.10 = (pred[1536]{0:T(1024)(128)(4,1)S(1)}, pred[1536]{0:T(1024)(128)(4,1)}, u32[]{:S(2)}) copy-start(pred[1536]{0:T(1024)(128)(4,1)} %get-tuple-element.11) | copy-start | bytes 4612
  27.2 77.2 %copy-start.11 = (pred[1536]{0:T(1024)(128)(4,1)S(1)}, pred[1536]{0:T(1024)(128)(4,1)}, u32[]{:S(2)}) copy-start(pred[1536]{0:T(1024)(128)(4,1)} %get-tuple-element.12) | copy-start | bytes 4612
  189.0 6.2 copy-start.7
  194.1 1.1 copy-start.2
  280.1 2.7 copy-start.1
  280.1 372.2 %all-reduce.3.cloned.1.call-start = ((), (), s32[]{:S(2)}) async-start(), calls=%async_computation.4 | async-start | bytes 4718592 | tf_op jit(solution)/shard_map/psum | solution.py:74
  289.2 99.0 %copy-start.5 = (bf16[512,64]{0,1:T(8,128)(2,1)S(1)}, bf16[512,64]{0,1:T(8,128)(2,1)}, u32[]{:S(2)}) copy-start(bf16[512,64]{0,1:T(8,128)(2,1)} %param.21) | copy-start | bytes 196612
  386.0 2.2 copy-start.3
Sparse Core Ops, SparseCore 0:
  11.2 83.8 all-gather.1
  280.3 105.6 reduce-scatter.1
  392.3 260.0 all-reduce.2
